TPU v7x, 32 devices: a whole 2x2x4 slice. The times are simulated.
32 devices in a mesh: group: 2 (over y), head: 4 (over z), req: 4 (over x, core).
Axes of the slice: x: 2, y: 2, z: 4, core: 2. Of those that a mesh axis runs over, the one named last changes fastest.
Arguments:
- x_input: bfloat16 [128, 8, 16384], P(('group', 'req'), None, 'head'), parts along dimension 0, may hold values from -6 to 6
- z_input: bfloat16 [128, 8, 16384], P(('group', 'req'), None, 'head'), parts along dimension 0, may hold values from -6 to 6
- bc_input: bfloat16 [128, 8, 4096], P(('group', 'req')), parts along dimension 0, may hold values from -6 to 6
- dt_input: float32 [128, 8, 256], P(('group', 'req'), None, 'head'), parts along dimension 0, may hold values from -6 to 6
- conv_x_state: bfloat16 [128, 3, 16384], P(('group', 'req'), None, 'head'), parts along dimension 0, may hold values from -6 to 6
- conv_bc_state: bfloat16 [128, 3, 4096], P(('group', 'req')), parts along dimension 0, may hold values from -6 to 6
- ssm_state: bfloat16 [128, 256, 64, 256], P(('group', 'req'), 'head'), parts along dimension 0, may hold values from -6 to 6
- accepted: int32 [128], P(('group', 'req')), parts along dimension 0, may hold values from 0 to 8
- next_owner: int32 [128], P('group'), parts along dimension 0, may hold values from 0 to 3, as said below
- conv_x_weight: float32 [4, 16384], P(None, 'head'), may hold values from -3 to 3
- conv_x_bias: float32 [16384], P('head'), may hold values from -3 to 3
- conv_bc_weight: float32 [4, 4096], replicated, may hold values from -3 to 3
- conv_bc_bias: float32 [4096], replicated, may hold values from -3 to 3
- dt_bias: float32 [256], P('head'), may hold values from -3 to 0
- a_log: float32 [256], P('head'), may hold values from -4 to 1
- d_skip: float32 [256], P('head'), may hold values from 0.5 to 1.5
- norm_gain: float32 [16384], P('head'), may hold values from 0.5 to 1.5
- out_weight: bfloat16 [16384, 8192], P('head'), may hold values from -0.0625 to 0.0625
Outputs:
- mixed: bfloat16 [128, 8, 8192], P(('group', 'req'), None, 'head'), parts along dimension 0
- new_ssm_state: bfloat16 [128, 256, 64, 256], P(('group', 'req'), 'head'), parts along dimension 0
- new_conv_x_state: bfloat16 [128, 3, 16384], P(('group', 'req'), None, 'head'), parts along dimension 0
- new_conv_bc_state: bfloat16 [128, 3, 4096], P(('group', 'req')), parts along dimension 0
There are 2 independent parts, one for each index of `group`. A program takes and returns all parts, laid end to end along the dimension named above; an argument that names none is the same for every part. Nothing has to cross between parts.
Inputs may be any that keep to these rules, and one draw needn't show every extreme that they name: Every index of req is next_owner of exactly 16 requests, and at most 8 of the requests of one index of req (requests i * 16 .. i * 16 + 15) share one next_owner.
All inputs are finite; a program needn't handle non-finite values.
Results may differ from a plain program's by a relative error of at most 0.0049.
Values may be sent and summed in bfloat16 or wider, within the bound.
No kernel may reach another device: no remote copies, remote signals or barrier semaphores. Data moves between devices by JAX's collectives and lax.ppermute only.
A program may use at most 576 MiB of HBM per device.

v0:
```python
import jax
import jax.numpy as jnp
from jax import lax
from jax.sharding import PartitionSpec as P

D = 8192
H = 256
P_SIZE = 64
N = 256
G = 8
K = 4
L = 8
epsilon = 1e-05
highest = lax.Precision.HIGHEST


def conv_window(history, inputs, weight, bias_vector):
    joined = jnp.concatenate([history, inputs], axis=1)
    widened = joined.astype(jnp.float32)
    accumulated = bias_vector[None, None, :] + weight[0][None, None, :] * widened[:, 0:L, :]
    for offset in range(1, K):
        accumulated = (
            accumulated + weight[offset][None, None, :] * widened[:, offset : offset + L, :]
        )
    return (jax.nn.silu(accumulated), joined)


def on_device(
    x_input,
    z_input,
    bc_input,
    dt_input,
    conv_x_state,
    conv_bc_state,
    ssm_state,
    accepted,
    next_owner,
    conv_x_weight,
    conv_x_bias,
    conv_bc_weight,
    conv_bc_bias,
    dt_bias,
    a_log,
    d_skip,
    norm_gain,
    out_weight,
):
    local_requests = x_input.shape[0]
    local_heads = dt_input.shape[2]
    head_index = lax.axis_index("head")
    req_index = lax.axis_index("req")
    all_requests = next_owner.shape[0]
    heads_group = H // G
    x_conv, x_joined = conv_window(conv_x_state, x_input, conv_x_weight, conv_x_bias)
    bc_conv, bc_joined = conv_window(conv_bc_state, bc_input, conv_bc_weight, conv_bc_bias)
    step_size = jax.nn.softplus(dt_input + dt_bias[None, None, :])
    log_decay = -jnp.exp(a_log)[None, None, :] * step_size
    global_heads = head_index * local_heads + jnp.arange(local_heads, dtype=jnp.int32)
    group_pick = (
        global_heads[:, None] // heads_group == jnp.arange(G, dtype=jnp.int32)[None, :]
    ).astype(jnp.float32)
    b_groups = bc_conv[:, :, : G * N].reshape(local_requests, L, G, N)
    c_groups = bc_conv[:, :, G * N :].reshape(local_requests, L, G, N)
    b_heads = jnp.einsum("rlgn,hg->rlhn", b_groups, group_pick, precision=highest)
    c_heads = jnp.einsum("rlgn,hg->rlhn", c_groups, group_pick, precision=highest)
    x_heads = x_conv.reshape(local_requests, L, local_heads, P_SIZE)
    initial = ssm_state.astype(jnp.float32)
    inclusive = jnp.cumsum(log_decay, axis=1)
    before = jnp.concatenate(
        [jnp.zeros((local_requests, 1, local_heads), jnp.float32), inclusive], axis=1
    )
    positions = jnp.arange(L, dtype=jnp.int32)
    causal = positions[:, None] >= positions[None, :]
    by_head = inclusive.transpose(0, 2, 1)
    differences = by_head[:, :, :, None] - by_head[:, :, None, :]
    pair_decay = jnp.exp(jnp.where(causal[None, None], differences, -jnp.inf))
    scores = jnp.einsum("rthn,rshn->rhts", c_heads, b_heads, precision=highest)
    weights = scores * pair_decay * step_size.transpose(0, 2, 1)[:, :, None, :]
    within = jnp.einsum("rhts,rshp->rthp", weights, x_heads, precision=highest)
    carried = jnp.exp(inclusive)[:, :, :, None] * jnp.einsum(
        "rhpn,rthn->rthp", initial, c_heads, precision=highest
    )
    y_values = within + carried + d_skip[None, None, :, None] * x_heads
    count_pick = (jnp.arange(L + 1, dtype=jnp.int32)[None, :] == accepted[:, None]).astype(
        jnp.float32
    )
    reached = jnp.einsum("ra,rah->rh", count_pick, before, precision=highest)
    valid = positions[None, :] < accepted[:, None]
    exponent = jnp.where(valid[:, :, None], reached[:, None, :] - inclusive, -jnp.inf)
    token_weight = jnp.exp(exponent) * step_size
    retained = jnp.exp(reached)[:, :, None, None] * initial + jnp.einsum(
        "rsh,rshp,rshn->rhpn", token_weight, x_heads, b_heads, precision=highest
    )
    retained = retained.astype(jnp.bfloat16)
    gated = y_values.reshape(local_requests, L, local_heads * P_SIZE) * jax.nn.silu(
        z_input.astype(jnp.float32)
    )
    blocks = gated.reshape(local_requests, L, local_heads, P_SIZE)
    inverse_rms = lax.rsqrt(jnp.mean(blocks * blocks, axis=3, keepdims=True) + epsilon)
    normed = (
        (blocks * inverse_rms).reshape(local_requests, L, local_heads * P_SIZE)
        * norm_gain[None, None, :]
    ).astype(jnp.bfloat16)
    partial_terms = jnp.dot(
        normed.reshape(local_requests * L, local_heads * P_SIZE),
        out_weight,
        preferred_element_type=jnp.float32,
    )
    share_width = D // lax.axis_size("head")
    summed = lax.psum(partial_terms, "head")
    share = lax.dynamic_slice_in_dim(summed, head_index * share_width, share_width, 1)
    mixed = share.astype(jnp.bfloat16).reshape(local_requests, L, share_width)
    window_rows = jnp.arange(K - 1 + L, dtype=jnp.int32)
    row_pick = (
        window_rows[None, None, :]
        == accepted[:, None, None] + jnp.arange(K - 1, dtype=jnp.int32)[None, :, None]
    ).astype(jnp.bfloat16)
    kept_x = jnp.einsum(
        "rkt,rtc->rkc", row_pick, x_joined, preferred_element_type=jnp.float32
    ).astype(jnp.bfloat16)
    kept_bc = jnp.einsum(
        "rkt,rtc->rkc", row_pick, bc_joined, preferred_element_type=jnp.float32
    ).astype(jnp.bfloat16)
    state_flat = retained.reshape(local_requests, -1)
    conv_x_flat = kept_x.reshape(local_requests, -1)
    conv_bc_flat = kept_bc.reshape(local_requests, -1)
    request_ids = jnp.arange(all_requests, dtype=jnp.int32)
    same_owner = next_owner[:, None] == next_owner[None, :]
    earlier = request_ids[None, :] < request_ids[:, None]
    position = jnp.sum((same_owner & earlier).astype(jnp.int32), axis=1)
    slot_rows = jnp.arange(local_requests, dtype=jnp.int32)
    arrive = (
        (next_owner[None, :] == req_index) & (position[None, :] == slot_rows[:, None])
    ).astype(jnp.bfloat16)
    new_state_flat = jnp.dot(
        arrive,
        lax.all_gather(state_flat, "req", axis=0, tiled=True),
        preferred_element_type=jnp.float32,
    ).astype(jnp.bfloat16)
    new_conv_x_flat = jnp.dot(
        arrive,
        lax.all_gather(conv_x_flat, "req", axis=0, tiled=True),
        preferred_element_type=jnp.float32,
    ).astype(jnp.bfloat16)
    new_conv_bc_flat = jnp.dot(
        arrive,
        lax.all_gather(conv_bc_flat, "req", axis=0, tiled=True),
        preferred_element_type=jnp.float32,
    ).astype(jnp.bfloat16)
    new_ssm_state = new_state_flat.reshape(retained.shape)
    new_conv_x_state = new_conv_x_flat.reshape(kept_x.shape)
    new_conv_bc_state = new_conv_bc_flat.reshape(kept_bc.shape)
    return (mixed, new_ssm_state, new_conv_x_state, new_conv_bc_state)


def solution(mesh):
    placed = (
        P(("group", "req"), None, "head"),
        P(("group", "req"), None, "head"),
        P(("group", "req"), None, None),
        P(("group", "req"), None, "head"),
        P(("group", "req"), None, "head"),
        P(("group", "req"), None, None),
        P(("group", "req"), "head", None, None),
        P(("group", "req")),
        P("group"),
        P(None, "head"),
        P("head"),
        P(),
        P(),
        P("head"),
        P("head"),
        P("head"),
        P("head"),
        P("head", None),
    )
    return jax.shard_map(
        on_device,
        mesh=mesh,
        in_specs=placed,
        out_specs=(
            P(("group", "req"), None, "head"),
            P(("group", "req"), "head", None, None),
            P(("group", "req"), None, "head"),
            P(("group", "req"), None, None),
        ),
        check_vma=False,
    )
```

profile of v0, /device:TPU:0, one launch (start us, length us, event | category | flops | bytes accessed | tf_op | source)
XLA Modules:
  0.0 1015.5 jit_solution(1302443822829279630)
XLA Ops:
  7.2 0.0 all-gather.8.cloned.1.call-start
  7.2 0.8 iota_add_fusion
  8.1 1.3 copy.48
  9.4 2.0 convolution_convert_fusion.3
  11.4 0.0 copy-start.13
  11.4 1.0 copy.73
  12.5 0.0 all-gather.8.cloned.1.call-update
  12.5 0.0 all-gather.6.cloned.1.call-start
  12.6 0.3 copy.47
  12.9 0.8 convolution_convert_fusion.4
  13.7 0.0 copy-start.5
  13.7 1.0 copy.72
  14.8 0.0 all-gather.6.cloned.1.call-update
  14.8 0.0 all-gather.4.cloned.1.call-start
  14.9 0.1 fusion.56
  14.9 0.1 iota_compare_fusion.4
  15.0 2.6 fusion.36
  17.6 0.0 copy-done.5
  17.7 0.0 copy-start.9
  17.7 0.0 copy-start.10
  17.7 0.0 copy-start.11
  17.7 2.7 fusion.35
  20.4 0.1 broadcast_multiply_fusion.1
  20.5 0.1 reduce_window_sum.11
  20.6 0.2 fusion.46
  20.9 0.1 exponential_multiply_fusion
  21.0 7.4 divide_multiply_fusion.1
  28.4 0.0 copy-start.12
  28.4 3.0 reshape.178
  31.4 0.0 copy-done.12
  31.4 7.0 divide_multiply_fusion
  38.5 0.0 copy-start.2
  38.5 1.2 fusion.75
  39.6 1.4 copy-done.2
  41.0 2.6 broadcast_multiply_fusion
  43.7 5.8 convolution_bitcast_fusion
  49.4 72.6 %add_convert_fusion = bf16[16,64,64,256]{3,2,1,0:T(8,128)(2,1)} fusion(bf16[16,64,64,256]{3,2,1,0:T(8,128)(2,1)} %param.24, f32[16,64]{1,0:T(8,128)S(1)} %exp.40, f32[16,8,64,256]{3,2,1,0:T(8,128)} %convolution_bitcast_fusion, f32[16,8,64,64]{3,2,1,0:T(8,128)} %broadcast_multiply_fusion), kind=kOutput, calls=%fused_computation.1 | convolution fusion | flops 1677721600 | bytes 77598720 | tf_op jit(solution)/shard_map/rsh,rshp,rshn->rhpn/dot_general | solution.py:91
  122.1 31.2 %copy.70 = bf16[2,8,4096,256]{3,1,2,0:T(8,128)(2,1)} copy(bf16[2,8,4096,256]{3,2,1,0:T(8,128)(2,1)} %bitcast.78) | data formatting | bytes 67108864
  153.3 0.0 all-gather.4.cloned.1.call-update
  153.3 1.0 copy.53
  154.3 0.2 copy.55
  154.5 0.2 copy.51
  154.7 8.9 convolution_bitcast_fusion.1
  163.6 21.0 %fusion.1 = f32[16,64,8,8]{3,2,1,0:T(8,128)} fusion(f32[16,8,64,256]{3,2,1,0:T(8,128)S(1)} %copy-done, f32[16,8,64,256]{3,2,1,0:T(8,128)} %convolution_bitcast_fusion.1), kind=kOutput, calls=%fused_computation.5 | convolution fusion | flops 201326592 | bytes 17039360 | tf_op jit(solution)/shard_map/rthn,rshn->rhts/dot_general | solution.py:77
  184.6 16.2 %fusion.9 = f32[16,64,64,8]{2,3,1,0:T(8,128)} fusion(f32[16,64,8,8]{3,2,1,0:T(8,128)} %fusion.1, f32[16,8,64,64]{3,2,1,0:T(8,128)} %reshape.178, f32[16,64,8]{2,1,0:T(8,128)} %copy.53, f32[16,64,8]{2,1,0:T(8,128)S(1)} %copy.51, pred[8,8]{1,0:T(8,128)(4,1)S(1)} %iota_compare_fusion.7), kind=kOutput, calls=%fused_computation.16 | convolution fusion | flops 50593792 | bytes 4522048 | tf_op jit(solution)/shard_map/rhts,rshp->rthp/dot_general | solution.py:79
  200.9 35.1 %fusion.7 = f32[16,8,64,64]{3,1,2,0:T(8,128)} fusion(f32[16,64,64,8]{2,3,1,0:T(8,128)} %fusion.9, f32[16,8,64,64]{3,2,1,0:T(8,128)} %reshape.178, bf16[16,64,64,256]{3,2,1,0:T(8,128)(2,1)} %param.24, f32[16,8,64,256]{3,2,1,0:T(8,128)S(1)} %copy-done.1, f32[64]{0:T(128)S(1)} %copy-done.14, f32[16,8,64]{1,2,0:T(8,128)S(1)} %copy.55), kind=kOutput, calls=%fused_computation.14 | convolution fusion | flops 1612709888 | bytes 48267520 | tf_op jit(solution)/shard_map/rhpn,rthn->rthp/dot_general | solution.py:80
  236.0 5.4 copy.58
  241.5 4.2 reshape.181
  245.7 1.9 fusion.74
  247.6 4.7 mul.209
  252.2 3.3 reduce_sum.18
  255.6 2.6 mul.210
  258.3 4.8 mul.211
  263.0 26.6 %fusion.38 = f32[128,8192]{1,0:T(8,128)} fusion(bf16[4096,8192]{1,0:T(8,128)(2,1)} %param.35, f32[16,8,4096]{2,1,0:T(8,128)} %mul.211, f32[4096]{0:T(1024)S(1)} %copy-done.8, f32[16,8,4096]{2,1,0:T(8,128)S(1)} %reshape.181, bf16[16,8,4096]{2,1,0:T(8,128)(2,1)S(1)} %copy-done.3), kind=kOutput, calls=%fused_computation.61 | convolution fusion | flops 8594653184 | bytes 76562432 | tf_op jit(solution)/shard_map/dot_general | solution.py:104
  289.7 0.2 convert_reduce_fusion
  289.9 150.2 %all-reduce.2 = bf16[128,8192]{1,0:T(8,128)(2,1)S(1)} all-reduce(f32[128,8192]{1,0:T(8,128)} %fusion.38), channel_id=1, replica_groups=mesh['group'=2,'head'=4,'req'=4] {'head'}, use_global_device_ids=true, to_apply=%region_2.3 | all-reduce | flops 1048576 | bytes 6291456 | tf_op jit(solution)/shard_map/psum | solution.py:110
  440.1 0.8 fusion.45
  440.9 1.7 convolution_convert_fusion.1
  442.6 0.8 copy.101
  443.4 1.7 convolution_convert_fusion.2
  445.1 0.8 copy.102
  445.9 485.2 %all-gather.4.cloned.1.call-done = bf16[64,1048576]{1,0:T(8,128)(2,1)} async-done(((bf16[16,1048576]{1,0:T(8,128)(2,1)}), bf16[64,1048576]{1,0:T(8,128)(2,1)}) %all-gather.4.cloned.1.call-update) | async-done | bytes 134217744 | tf_op jit(solution)/shard_map/all_gather | solution.py:137
  931.1 54.6 %convolution_convert_fusion = bf16[16,1048576]{1,0:T(8,128)(2,1)} fusion(bf16[64,1048576]{1,0:T(8,128)(2,1)} %all-gather.4.cloned.1.call-done, s32[64]{0:T(128)S(1)} %convert_reduce_fusion, pred[64]{0:T(512)(128)(4,1)S(1)} %broadcast_compare_fusion), kind=kOutput, calls=%fused_computation | convolution fusion | flops 2164262912 | bytes 167772480 | tf_op jit(solution)/shard_map/dot_general | solution.py:135
  985.7 23.1 %copy.71 = bf16[2,8,4096,256]{3,2,1,0:T(8,128)(2,1)} copy(bf16[2,8,4096,256]{3,1,2,0:T(8,128)(2,1)} %bitcast.79) | data formatting | bytes 67108864
  (36 shorter events, 0.2 us)
Async XLA Ops:
  7.2 5.4 copy-start.6
  7.2 5.7 copy-start.4
  7.2 433.7 %all-gather.8.cloned.1.call-start = ((), (), s32[]{:S(2)}) async-start(), calls=%async_computation.2 | async-start | bytes 1966080 | tf_op jit(solution)/shard_map/all_gather | solution.py:147
  11.4 3.4 copy-start.13
  12.5 430.9 %all-gather.6.cloned.1.call-start = ((), (), s32[]{:S(2)}) async-start(), calls=%async_computation.1 | async-start | bytes 1966080 | tf_op jit(solution)/shard_map/all_gather | solution.py:142
  13.7 3.9 copy-start.5
  14.8 916.3 %all-gather.4.cloned.1.call-start = ((), (), s32[]{:S(2)}) async-start(), calls=%async_computation | async-start | bytes 167772160 | tf_op jit(solution)/shard_map/all_gather | solution.py:137
  17.7 2.8 copy-start.16
  17.7 2.8 copy-start.7
  17.7 2.8 copy-start.15
  17.7 3.1 copy-start.9
  17.7 3.2 copy-start.10
  17.7 3.4 copy-start.11
  28.4 3.0 copy-start.12
  38.5 2.6 copy-start.2
  154.7 8.9 copy-start
  184.6 16.2 %copy-start.1 = (f32[16,8,64,256]{3,2,1,0:T(8,128)S(1)}, f32[16,8,64,256]{3,2,1,0:T(8,128)}, u32[]{:S(2)}) copy-start(f32[16,8,64,256]{3,2,1,0:T(8,128)} %convolution_bitcast_fusion.1) | copy-start | bytes 25165828
  184.6 16.2 %copy-start.14 = (f32[64]{0:T(128)S(1)}, f32[64]{0:T(128)}, u32[]{:S(2)}) copy-start(f32[64]{0:T(128)} %param.33) | copy-start | bytes 772
  241.5 4.2 copy-start.3
  258.3 4.8 copy-start.8
  263.0 26.6 %copy-start.17 = (s32[64]{0:T(128)S(1)}, s32[64]{0:T(128)}, u32[]{:S(2)}) copy-start(s32[64]{0:T(128)} %param.26) | copy-start | bytes 772
Sparse Core Ops, SparseCore 0:
  12.6 22.3 all-gather.7
  37.1 19.6 all-gather.5
  153.4 777.6 all-gather.3
where the time goes:
time: 1020 us
  waiting for transfers between devices  485 us (48%)
  matrix products  247 us (24%)
  blocking collectives  150 us (15%)
  local copies, waits for them, and re-layouts  89.3 us (9%)
  other arithmetic  29 us (3%)
  between operations  14.3 us (1%)
    all_gather x1, waiting for transfers between devices, on_device(): lax.all_gather(state_flat, 'req', axis=0, tiled=True)  485 us
    psum x1, blocking collectives, on_device(): summed = lax.psum(partial_terms, 'head')  150 us
    dot_general x1, matrix products, on_device(): jnp.einsum('rsh,rshp,rshn->rhpn', token_weight, x_heads, b_heads, precisi...  72.6 us
    unnamed x42, local copies, waits for them, and re-layouts  59.5 us
    dot_general x1, matrix products, on_device(): jnp.dot(arrive, lax.all_gather(state_flat, 'req', axis=0, tiled=True), pr...  54.6 us
    dot_general x1, matrix products, on_device(): jnp.einsum('rhpn,rthn->rthp', initial, c_heads, precision=highest)  35.1 us
    dot_general x1, matrix products, on_device(): jnp.dot(normed.reshape(local_requests * L, local_heads * P_SIZE), out_wei...  26.6 us
    dot_general x1, matrix products, on_device(): scores = jnp.einsum('rthn,rshn->rhts', c_heads, b_heads, precision=highest)  21 us
  transfers between devices with their start and end apart: 3, of which 1 were waited for; matrix products, arithmetic and copies ran while one was open for 28% of the time, Pallas kernels for 0%

commit v1 on v0

--- a/solution.py
+++ b/solution.py
@@ -107,7 +107,7 @@
         preferred_element_type=jnp.float32,
     )
     share_width = D // lax.axis_size("head")
-    summed = lax.psum(partial_terms, "head")
+    summed = jnp.sum(lax.all_gather(partial_terms, "head"), axis=0)
     share = lax.dynamic_slice_in_dim(summed, head_index * share_width, share_width, 1)
     mixed = share.astype(jnp.bfloat16).reshape(local_requests, L, share_width)
     window_rows = jnp.arange(K - 1 + L, dtype=jnp.int32)

time: 1020 us -> 1320 us (1.29)
  waiting for transfers between devices: 485 us -> 942 us
  blocking collectives: 150 us -> 0 us
    all_gather x1, waiting for transfers between devices: 485 us -> 766 us  [on_device(): lax.all_gather(state_flat, 'req', axis=0, tiled=True)]
    all_gather x0 -> x1, waiting for transfers between devices: none -> 176 us  [on_device(): summed = jnp.sum(lax.all_gather(partial_terms, 'head'), axis=0)]
    psum x1 -> x0, blocking collectives: 150 us -> none  [on_device(): summed = lax.psum(partial_terms, 'head')]
    unnamed x42 -> x40, local copies, waits for them, and re-layouts: 59.5 us -> 58.7 us
  transfers between devices with their start and end apart: 3 -> 4, of which waited for: 1 -> 2; matrix products, arithmetic and copies ran while one was open for 28% -> 21% of each run, Pallas kernels for 0% -> 0%
where the time goes in v1:
time: 1320 us
  waiting for transfers between devices  942 us (71%)
  matrix products  235 us (18%)
  local copies, waits for them, and re-layouts  86.5 us (7%)
  other arithmetic  38.1 us (3%)
  between operations  14.5 us (1%)
    all_gather x1, waiting for transfers between devices, on_device(): lax.all_gather(state_flat, 'req', axis=0, tiled=True)  766 us
    all_gather x1, waiting for transfers between devices, on_device(): summed = jnp.sum(lax.all_gather(partial_terms, 'head'), axis=0)  176 us
    dot_general x1, matrix products, on_device(): jnp.einsum('rsh,rshp,rshn->rhpn', token_weight, x_heads, b_heads, precisi...  72.4 us
    unnamed x40, local copies, waits for them, and re-layouts  58.7 us
    dot_general x1, matrix products, on_device(): jnp.dot(arrive, lax.all_gather(state_flat, 'req', axis=0, tiled=True), pr...  54.6 us
    dot_general x1, matrix products, on_device(): jnp.einsum('rhpn,rthn->rthp', initial, c_heads, precision=highest)  31.9 us
    dot_general x1, matrix products, on_device(): jnp.dot(normed.reshape(local_requests * L, local_heads * P_SIZE), out_wei...  26.6 us
  transfers between devices with their start and end apart: 4, of which 2 were waited for; matrix products, arithmetic and copies ran while one was open for 21% of the time, Pallas kernels for 0%

profile of v1, /device:TPU:0, one launch (start us, length us, event | category | flops | bytes accessed | tf_op | source)
XLA Modules:
  0.0 1317.0 jit_solution(12811983450559123282)
XLA Ops:
  7.2 0.0 all-gather.10.cloned.1.call-start
  7.2 0.8 iota_add_fusion
  8.1 1.3 copy.48
  9.4 2.0 convolution_convert_fusion.3
  11.4 0.0 copy-start.12
  11.4 1.0 copy.73
  12.5 0.0 all-gather.10.cloned.1.call-update
  12.5 0.0 all-gather.8.cloned.1.call-start
  12.6 0.3 copy.47
  12.9 0.8 convolution_convert_fusion.4
  13.7 0.0 copy-start.4
  13.7 1.0 copy.72
  14.8 0.0 all-gather.8.cloned.1.call-update
  14.8 0.3 all-gather.12.cloned.1.call-start
  15.1 0.1 fusion.56
  15.2 0.1 iota_compare_fusion.4
  15.2 2.6 fusion.36
  17.9 0.0 copy-start.6
  17.9 0.0 copy-start.14
  17.9 0.0 copy-start.10
  17.9 2.7 fusion.35
  20.8 0.1 broadcast_multiply_fusion.1
  20.8 0.1 reduce_window_sum.11
  20.9 0.2 fusion.46
  21.1 0.1 exponential_multiply_fusion
  21.2 1.0 copy.53
  22.2 0.2 copy.55
  22.4 0.2 copy.51
  22.7 7.0 divide_multiply_fusion.1
  29.7 3.0 reshape.178
  32.7 7.1 divide_multiply_fusion
  39.8 0.2 fusion.75
  40.1 3.5 convolution_bitcast_fusion
  43.6 6.0 convolution_bitcast_fusion.1
  49.6 19.4 %fusion.1 = f32[16,64,8,8]{3,2,1,0:T(8,128)} fusion(f32[16,8,64,256]{3,2,1,0:T(8,128)S(1)} %convolution_bitcast_fusion, f32[16,8,64,256]{3,2,1,0:T(8,128)} %convolution_bitcast_fusion.1), kind=kOutput, calls=%fused_computation.5 | convolution fusion | flops 201326592 | bytes 17039360 | tf_op jit(solution)/shard_map/rthn,rshn->rhts/dot_general | solution.py:77
  69.0 14.4 %fusion.9 = f32[16,64,64,8]{2,3,1,0:T(8,128)} fusion(f32[16,64,8,8]{3,2,1,0:T(8,128)} %fusion.1, f32[16,8,64,64]{3,2,1,0:T(8,128)} %reshape.178, f32[16,64,8]{2,1,0:T(8,128)} %copy.53, f32[16,64,8]{2,1,0:T(8,128)S(1)} %copy.51, pred[8,8]{1,0:T(8,128)(4,1)S(1)} %iota_compare_fusion.7), kind=kOutput, calls=%fused_computation.16 | convolution fusion | flops 50593792 | bytes 4522048 | tf_op jit(solution)/shard_map/rhts,rshp->rthp/dot_general | solution.py:79
  83.4 31.9 %fusion.7 = f32[16,8,64,64]{3,1,2,0:T(8,128)} fusion(f32[16,64,64,8]{2,3,1,0:T(8,128)} %fusion.9, f32[16,8,64,64]{3,2,1,0:T(8,128)} %reshape.178, bf16[16,64,64,256]{3,2,1,0:T(8,128)(2,1)} %param.24, f32[16,8,64,256]{3,2,1,0:T(8,128)S(1)} %copy-done.1, f32[64]{0:T(128)S(1)} %copy-done.13, f32[16,8,64]{1,2,0:T(8,128)S(1)} %copy.55), kind=kOutput, calls=%fused_computation.14 | convolution fusion | flops 1612709888 | bytes 48267520 | tf_op jit(solution)/shard_map/rhpn,rthn->rthp/dot_general | solution.py:80
  115.3 4.9 copy.58
  120.2 3.8 reshape.181
  124.0 1.9 fusion.74
  125.9 4.6 mul.209
  130.5 3.3 reduce_sum.27
  133.8 2.6 mul.210
  136.5 4.8 mul.211
  141.3 26.6 %fusion.38 = f32[128,8192]{1,0:T(8,128)} fusion(bf16[4096,8192]{1,0:T(8,128)(2,1)} %param.35, f32[16,8,4096]{2,1,0:T(8,128)} %mul.211, f32[4096]{0:T(1024)S(1)} %copy-done.7, f32[16,8,4096]{2,1,0:T(8,128)S(1)} %reshape.181, bf16[16,8,4096]{2,1,0:T(8,128)(2,1)S(1)} %copy-done.2), kind=kOutput, calls=%fused_computation.61 | convolution fusion | flops 8594653184 | bytes 76562432 | tf_op jit(solution)/shard_map/dot_general | solution.py:104
  167.9 0.0 all-gather.12.cloned.1.call-update
  167.9 0.0 all-gather.6.cloned.1.call-start
  168.0 4.2 broadcast_multiply_fusion
  172.2 72.4 %add_convert_fusion = bf16[16,64,64,256]{3,2,1,0:T(8,128)(2,1)} fusion(bf16[16,64,64,256]{3,2,1,0:T(8,128)(2,1)} %param.24, f32[16,64]{1,0:T(8,128)S(1)} %exp.40, f32[16,8,64,256]{3,2,1,0:T(8,128)} %copy-done, f32[16,8,64,64]{3,2,1,0:T(8,128)} %broadcast_multiply_fusion), kind=kOutput, calls=%fused_computation.1 | convolution fusion | flops 1677721600 | bytes 77598720 | tf_op jit(solution)/shard_map/rsh,rshp,rshn->rhpn/dot_general | solution.py:91
  244.6 31.2 %copy.70 = bf16[2,8,4096,256]{3,1,2,0:T(8,128)(2,1)} copy(bf16[2,8,4096,256]{3,2,1,0:T(8,128)(2,1)} %bitcast.79) | data formatting | bytes 67108864
  275.8 0.0 all-gather.6.cloned.1.call-update
  275.8 0.6 copy-done.16
  276.5 0.2 convert_reduce_fusion
  276.7 0.0 all-gather.10.cloned.1.call-done
  276.7 1.7 convolution_convert_fusion.1
  278.4 0.8 copy.101
  279.2 1.7 convolution_convert_fusion.2
  280.9 0.8 copy.102
  281.7 175.9 %all-gather.12.cloned.1.call-done = f32[512,8192]{1,0:T(8,128)} async-done(((f32[128,8192]{1,0:T(8,128)}), f32[512,8192]{1,0:T(8,128)}) %all-gather.12.cloned.1.call-update) | async-done | bytes 16777232 | tf_op jit(solution)/shard_map/all_gather | solution.py:110
  457.6 7.8 reduce_sum.28
  465.4 0.8 fusion.45
  466.2 766.1 %all-gather.6.cloned.1.call-done = bf16[64,1048576]{1,0:T(8,128)(2,1)} async-done(((bf16[16,1048576]{1,0:T(8,128)(2,1)}), bf16[64,1048576]{1,0:T(8,128)(2,1)}) %all-gather.6.cloned.1.call-update) | async-done | bytes 134217744 | tf_op jit(solution)/shard_map/all_gather | solution.py:137
  1232.3 54.6 %convolution_convert_fusion = bf16[16,1048576]{1,0:T(8,128)(2,1)} fusion(bf16[64,1048576]{1,0:T(8,128)(2,1)} %all-gather.6.cloned.1.call-done, s32[64]{0:T(128)S(1)} %convert_reduce_fusion, pred[64]{0:T(512)(128)(4,1)S(1)} %broadcast_compare_fusion), kind=kOutput, calls=%fused_computation | convolution fusion | flops 2164262912 | bytes 167772480 | tf_op jit(solution)/shard_map/dot_general | solution.py:135
  1286.9 23.1 %copy.71 = bf16[2,8,4096,256]{3,2,1,0:T(8,128)(2,1)} copy(bf16[2,8,4096,256]{3,1,2,0:T(8,128)(2,1)} %bitcast.80) | data formatting | bytes 67108864
  (37 shorter events, 0.2 us)
Async XLA Ops:
  7.2 5.4 copy-start.5
  7.2 5.7 copy-start.3
  7.2 269.5 %all-gather.10.cloned.1.call-start = ((), (), s32[]{:S(2)}) async-start(), calls=%async_computation.2 | async-start | bytes 1966080 | tf_op jit(solution)/shard_map/all_gather | solution.py:147
  11.4 3.7 copy-start.12
  12.5 266.7 %all-gather.8.cloned.1.call-start = ((), (), s32[]{:S(2)}) async-start(), calls=%async_computation.1 | async-start | bytes 1966080 | tf_op jit(solution)/shard_map/all_gather | solution.py:142
  13.7 4.1 copy-start.4
  14.8 442.8 %all-gather.12.cloned.1.call-start = ((), (), s32[]{:S(2)}) async-start(), calls=%async_computation.3 | async-start | bytes 20971520 | tf_op jit(solution)/shard_map/all_gather | solution.py:110
  17.9 2.8 copy-start.15
  17.9 2.8 copy-start.8
  17.9 2.8 copy-start.9
  17.9 2.9 copy-start.6
  17.9 2.9 copy-start.14
  17.9 4.8 copy-start.10
  29.7 3.0 copy-start.11
  43.5 6.0 copy-start
  69.0 14.4 %copy-start.1 = (f32[16,8,64,256]{3,2,1,0:T(8,128)S(1)}, f32[16,8,64,256]{3,2,1,0:T(8,128)}, u32[]{:S(2)}) copy-start(f32[16,8,64,256]{3,2,1,0:T(8,128)} %convolution_bitcast_fusion.1) | copy-start | bytes 25165828
  69.0 14.4 %copy-start.13 = (f32[64]{0:T(128)S(1)}, f32[64]{0:T(128)}, u32[]{:S(2)}) copy-start(f32[64]{0:T(128)} %param.33) | copy-start | bytes 772
  120.2 3.8 copy-start.2
  136.5 4.8 copy-start.7
  167.9 1064.4 %all-gather.6.cloned.1.call-start = ((), (), s32[]{:S(2)}) async-start(), calls=%async_computation | async-start | bytes 167772160 | tf_op jit(solution)/shard_map/all_gather | solution.py:137
  275.8 0.7 copy-start.16
Sparse Core Ops, SparseCore 0:
  12.6 22.3 all-gather.9
  37.1 19.6 all-gather.7
  168.1 289.4 all-gather.11
  459.0 773.2 all-gather.5
